TPU v7x, 256 devices: a whole 4x4x8 slice. The times are simulated.
256 devices in a mesh: runs: 32 (over y, x, core), cells: 8 (over z).
Axes of the slice: x: 4, y: 4, z: 8, core: 2. Of those that a mesh axis runs over, the one named last changes fastest.
Arguments:
- train_depth: bfloat16 [16384, 32768], P('runs', 'cells'), may hold values from -6 to 6
- train_basis: bfloat16 [16384, 512], P('runs', 'cells'), may hold values from -6 to 6
- sample_basis: bfloat16 [16384, 512], P('runs', 'cells'), may hold values from -0.25 to 0.25
- gram_inverse: float32 [512, 512], replicated, may hold values from -8 to 8
Outputs:
- peak_depth: bfloat16 [16384, 32768], P('runs', 'cells')
All inputs are finite; a program needn't handle non-finite values.
Results may differ from a plain program's by a relative error of at most 0.0049.
Values may be sent and summed in bfloat16 or wider, within the bound.
No kernel may reach another device: no remote copies, remote signals or barrier semaphores. Data moves between devices by JAX's collectives and lax.ppermute only.
A program may use at most 64 MiB of HBM per device.

v0:
```python
import math

import jax
import jax.numpy as jnp
from jax import lax
from jax.sharding import PartitionSpec as P


def per_device(train_depth, train_basis, sample_basis, gram_inverse):
    train_full, sample_full = (
        lax.all_gather(train_basis, "cells", axis=1, tiled=True),
        lax.all_gather(sample_basis, "cells", axis=1, tiled=True),
    )
    total_runs = train_full.shape[0] * lax.axis_size("runs")
    norm_scale = 1.0 / math.sqrt(total_runs)
    partial_moments = lax.dot_general(
        train_full, train_depth, (((0,), (0,)), ((), ())), preferred_element_type=jnp.float32
    )
    moments = lax.psum(partial_moments, "runs") * norm_scale
    coeffs = jnp.dot(gram_inverse, moments, precision=lax.Precision.HIGHEST).astype(jnp.bfloat16)
    peak_depth = jnp.dot(sample_full, coeffs, preferred_element_type=jnp.float32).astype(
        jnp.bfloat16
    )
    return peak_depth


def solution(mesh):
    in_specs = (P("runs", "cells"), P("runs", "cells"), P("runs", "cells"), P())
    out_specs = P("runs", "cells")
    return jax.shard_map(
        per_device, mesh=mesh, in_specs=in_specs, out_specs=out_specs, check_vma=False
    )
```

profile of v0, /device:TPU:1, one launch (start us, length us, event | category | flops | bytes accessed | tf_op | source)
XLA Modules:
  0.0 220.2 jit_solution(13834818411331468858)
XLA Ops:
  6.5 0.0 copy-start
  6.5 0.0 all-reduce.2.cloned.1.call-start
  6.5 24.1 %all_gather.6 = bf16[512,512]{0,1:T(8,128)(2,1)S(1)} all-gather(bf16[512,64]{0,1:T(8,128)(2,1)} %param.5), channel_id=1, replica_groups=mesh['runs'=32,'cells'=8] {'cells'}, dimensions={1}, use_global_device_ids=true | all-gather | bytes 589824 | tf_op jit(solution)/shard_map/all_gather | solution.py:11
  30.6 7.8 %fusion.8 = f32[512,4096]{1,0:T(8,128)} fusion(bf16[512,512]{0,1:T(8,128)(2,1)S(1)} %all_gather.6, bf16[512,4096]{1,0:T(8,128)(2,1)} %param.4), kind=kOutput, calls=%fused_computation.7 | convolution fusion | flops 2147483648 | bytes 13107200 | tf_op jit(solution)/shard_map/dot_general | solution.py:16
  38.4 0.0 copy-start.1
  38.4 0.0 all-reduce.2.cloned.1.call-update
  38.5 0.8 copy-done.1
  39.3 19.5 %all_gather.7 = bf16[512,512]{0,1:T(8,128)(2,1)S(1)} all-gather(bf16[512,64]{0,1:T(8,128)(2,1)S(1)} %copy-done.1), channel_id=1, replica_groups=mesh['runs'=32,'cells'=8] {'cells'}, dimensions={1}, use_global_device_ids=true | all-gather | bytes 589824 | tf_op jit(solution)/shard_map/all_gather | solution.py:12
  58.7 115.6 %all-reduce.2.cloned.1.call-done = f32[512,4096]{1,0:T(8,128)} async-done(((f32[512,4096]{1,0:T(8,128)}), f32[512,4096]{1,0:T(8,128)}) %all-reduce.2.cloned.1.call-update) | async-done | bytes 8388624 | tf_op jit(solution)/shard_map/psum | solution.py:19
  174.3 0.0 copy-done
  174.3 28.4 %fusion.2 = bf16[4096,512]{1,0:T(8,128)(2,1)S(1)} fusion(f32[512,512]{1,0:T(8,128)S(1)} %copy-done, f32[512,4096]{1,0:T(8,128)} %all-reduce.2.cloned.1.call-done), kind=kOutput, calls=%fused_computation.2 | convolution fusion | flops 12889096192 | bytes 13631488 | tf_op jit(solution)/shard_map/dot_general | solution.py:20
  202.7 4.3 %fusion.5 = bf16[512,4096]{0,1:T(8,128)(2,1)} fusion(bf16[4096,512]{1,0:T(8,128)(2,1)S(1)} %fusion.2, bf16[512,512]{0,1:T(8,128)(2,1)S(1)} %all_gather.7), kind=kOutput, calls=%fused_computation.4 | convolution fusion | flops 2149580800 | bytes 8912896 | tf_op jit(solution)/shard_map/dot_general | solution.py:21
  207.0 6.3 %copy.5 = bf16[512,4096]{1,0:T(8,128)(2,1)} copy(bf16[512,4096]{0,1:T(8,128)(2,1)} %fusion.5) | data formatting | bytes 8388608 | tf_op jit(solution)/shard_map/convert_element_type | solution.py:21
Async XLA Ops:
  6.5 167.8 %copy-start = (f32[512,512]{1,0:T(8,128)S(1)}, f32[512,512]{1,0:T(8,128)}, u32[]{:S(2)}) copy-start(f32[512,512]{1,0:T(8,128)} %param.7) | copy-start | bytes 3145732
  6.5 167.8 %all-reduce.2.cloned.1.call-start = ((), (), s32[]{:S(2)}) async-start(), calls=%async_computation | async-start | bytes 16777216 | tf_op jit(solution)/shard_map/psum | solution.py:19
  38.4 0.8 copy-start.1
Sparse Core Ops, SparseCore 0:
  38.6 135.6 all-reduce.1
where the time goes:
time: 220 us
  waiting for transfers between devices  116 us (53%)
  blocking collectives  43.5 us (20%)
  matrix products  40.5 us (18%)
  between operations  13.4 us (6%)
  local copies, waits for them, and re-layouts  7.13 us (3%)
    psum x1, waiting for transfers between devices, per_device(): moments = lax.psum(partial_moments, 'runs') * norm_scale  116 us
    dot_general x1, matrix products, per_device(): jnp.dot(gram_inverse, moments, precision=lax.Precision.HIGHEST)  28.4 us
    all_gather x1, blocking collectives, per_device(): lax.all_gather(train_basis, 'cells', axis=1, tiled=True)  24.1 us
    all_gather x1, blocking collectives, per_device(): lax.all_gather(sample_basis, 'cells', axis=1, tiled=True)  19.5 us
    dot_general x1, matrix products, per_device(): lax.dot_general(train_full, train_depth, (((0,), (0,)), ((), ())), prefer...  7.84 us
    convert_element_type x1, local copies, waits for them, and re-layouts, per_device(): jnp.dot(sample_full, coeffs, preferred_element_type=jnp.float32)  6.32 us
  transfers between devices with their start and end apart: 1, of which 1 were waited for; matrix products, arithmetic and copies ran while one was open for 0% of the time, Pallas kernels for 0%

commit v1 on v0

v1 whole, which is shorter than its diff:
```python
import math

import jax
import jax.numpy as jnp
from jax import lax
from jax.sharding import PartitionSpec as P


def per_device(train_depth, train_basis, sample_basis, gram_inverse):
    terms_here = train_basis.shape[1]
    n_cells = lax.axis_size("cells")
    total_runs = train_depth.shape[0] * lax.axis_size("runs")
    norm_scale = 1.0 / math.sqrt(total_runs)
    both = jnp.concatenate([train_basis, sample_basis], axis=1).T
    both_full = lax.all_gather(both, "cells", axis=0, tiled=False)
    train_t = both_full[:, :terms_here, :].reshape(n_cells * terms_here, -1)
    sample_t = both_full[:, terms_here:, :].reshape(n_cells * terms_here, -1)
    partial_t = lax.dot_general(
        train_depth, train_t, (((0,), (1,)), ((), ())), preferred_element_type=jnp.float32
    )
    moments_t = lax.psum_scatter(partial_t, "runs", scatter_dimension=0, tiled=True) * norm_scale
    coeffs_t = lax.dot_general(
        moments_t, gram_inverse, (((1,), (1,)), ((), ())), precision=lax.Precision.HIGHEST
    ).astype(jnp.bfloat16)
    coeffs_full_t = lax.all_gather(coeffs_t, "runs", axis=0, tiled=True)
    peak_depth = lax.dot_general(
        sample_t, coeffs_full_t, (((0,), (1,)), ((), ())), preferred_element_type=jnp.float32
    ).astype(jnp.bfloat16)
    return peak_depth


def solution(mesh):
    in_specs = (P("runs", "cells"), P("runs", "cells"), P("runs", "cells"), P())
    out_specs = P("runs", "cells")
    return jax.shard_map(
        per_device, mesh=mesh, in_specs=in_specs, out_specs=out_specs, check_vma=False
    )
```

time: 220 us -> 227 us (1.032)
  waiting for transfers between devices: 116 us -> 193 us
  blocking collectives: 43.5 us -> 0 us
  matrix products: 40.5 us -> 17.3 us
  local copies, waits for them, and re-layouts: 7.13 us -> 1.27 us
    psum x1 -> x0, waiting for transfers between devices: 116 us -> none  [per_device(): moments = lax.psum(partial_moments, 'runs') * norm_scale]
    reduce_scatter x0 -> x1, waiting for transfers between devices: none -> 102 us  [per_device(): lax.psum_scatter(partial_t, 'runs', scatter_dimension=0, tiled=True)]
    all_gather x0 -> x2, waiting for transfers between devices: none -> 90.8 us  [the longest x1 52.7 us: per_device(): coeffs_full_t = lax.all_gather(coeffs_t, 'runs', axis=0, tiled=True)]
    all_gather x2 -> x0, blocking collectives: 43.5 us -> none  [the longest x1 24.1 us: per_device(): lax.all_gather(train_basis, 'cells', axis=1, tiled=True)]
    dot_general x3, matrix products: 40.5 us -> 17.3 us  [the longest x1 7.84 us: per_device(): lax.dot_general(train_depth, train_t, (((0,), (1,)), ((), ())), preferred...]
    convert_element_type x1 -> x0, local copies, waits for them, and re-layouts: 6.32 us -> none  [per_device(): jnp.dot(sample_full, coeffs, preferred_element_type=jnp.float32)]
  transfers between devices with their start and end apart: 1 -> 3, of which waited for: 1 -> 3; matrix products, arithmetic and copies ran while one was open for 0% -> 0% of each run, Pallas kernels for 0% -> 0%
where the time goes in v1:
time: 227 us; the launch traced here: 226 us
  waiting for transfers between devices  193 us (85%)
  matrix products  17.3 us (8%)
  between operations  13.1 us (6%)
    reduce_scatter x1, waiting for transfers between devices, per_device(): lax.psum_scatter(partial_t, 'runs', scatter_dimension=0, tiled=True)  102 us
    all_gather x1, waiting for transfers between devices, per_device(): coeffs_full_t = lax.all_gather(coeffs_t, 'runs', axis=0, tiled=True)  52.7 us
    all_gather x1, waiting for transfers between devices, per_device(): both_full = lax.all_gather(both, 'cells', axis=0, tiled=False)  38.1 us
    dot_general x1, matrix products, per_device(): lax.dot_general(train_depth, train_t, (((0,), (1,)), ((), ())), preferred...  7.84 us
    dot_general x1, matrix products, per_device(): lax.dot_general(sample_t, coeffs_full_t, (((0,), (1,)), ((), ())), prefer...  6.6 us
  transfers between devices with their start and end apart: 3, of which 3 were waited for; matrix products, arithmetic and copies ran while one was open for 0% of the time, Pallas kernels for 0%

profile of v1, /device:TPU:1, one launch (start us, length us, event | category | flops | bytes accessed | tf_op | source)
XLA Modules:
  0.0 226.3 jit_solution(17582883952233589478)
XLA Ops:
  6.5 0.0 copy-start
  6.5 0.0 all-gather.6.cloned.1.call-start
  6.5 1.6 maximum_bitcast_fusion
  8.2 0.0 all-gather.6.cloned.1.call-update
  8.2 0.0 reduce-scatter.2.cloned.1.call-start
  8.2 38.1 %all-gather.6.cloned.1.call-done = bf16[1024,512]{1,0:T(8,128)(2,1)} async-done(((bf16[128,512]{1,0:T(8,128)(2,1)}), bf16[1024,512]{1,0:T(8,128)(2,1)}) %all-gather.6.cloned.1.call-update) | async-done | bytes 1048592 | tf_op jit(solution)/shard_map/all_gather | solution.py:15
  46.3 1.3 fusion.3
  47.6 7.8 %convolution_bitcast_fusion = f32[4096,512]{0,1:T(8,128)} fusion(bf16[512,512]{1,0:T(8,128)(2,1)S(1)} %bitcast.12, bf16[512,4096]{1,0:T(8,128)(2,1)} %param.4), kind=kOutput, calls=%fused_computation | convolution fusion | flops 2147483648 | bytes 13107200 | tf_op jit(solution)/shard_map/dot_general | solution.py:18
  55.4 0.0 reduce-scatter.2.cloned.1.call-update
  55.5 0.0 all-gather.4.cloned.1.call-start
  55.5 102.1 %reduce-scatter.2.cloned.1.call-done = f32[128,512]{0,1:T(8,128)} async-done(((f32[4096,512]{0,1:T(8,128)}), f32[128,512]{0,1:T(8,128)}) %reduce-scatter.2.cloned.1.call-update) | async-done | bytes 262160 | tf_op jit(solution)/shard_map/reduce_scatter | solution.py:21
  157.6 0.0 copy-done
  157.7 2.9 %convolution_convert_fusion.1 = bf16[128,512]{1,0:T(8,128)(2,1)} fusion(f32[512,512]{1,0:T(8,128)S(1)} %copy-done, f32[128,512]{0,1:T(8,128)} %reduce-scatter.2.cloned.1.call-done), kind=kOutput, calls=%fused_computation.2 | convolution fusion | flops 402784256 | bytes 1441792 | tf_op jit(solution)/shard_map/dot_general | solution.py:22
  160.5 0.0 all-gather.4.cloned.1.call-update
  160.5 52.7 %all-gather.4.cloned.1.call-done = bf16[4096,512]{1,0:T(8,128)(2,1)} async-done(((bf16[128,512]{1,0:T(8,128)(2,1)}), bf16[4096,512]{1,0:T(8,128)(2,1)}) %all-gather.4.cloned.1.call-update) | async-done | bytes 4194320 | tf_op jit(solution)/shard_map/all_gather | solution.py:25
  213.2 6.6 %convolution_convert_fusion = bf16[512,4096]{1,0:T(8,128)(2,1)} fusion(bf16[512,512]{1,0:T(8,128)(2,1)S(1)} %bitcast.14, bf16[4096,512]{1,0:T(8,128)(2,1)} %all-gather.4.cloned.1.call-done), kind=kOutput, calls=%fused_computation.1 | convolution fusion | flops 2149580800 | bytes 8912896 | tf_op jit(solution)/shard_map/dot_general | solution.py:26
Async XLA Ops:
  6.5 151.1 %copy-start = (f32[512,512]{1,0:T(8,128)S(1)}, f32[512,512]{1,0:T(8,128)}, u32[]{:S(2)}) copy-start(f32[512,512]{1,0:T(8,128)} %param.7) | copy-start | bytes 3145732
  6.5 39.8 %all-gather.6.cloned.1.call-start = ((), (), s32[]{:S(2)}) async-start(), calls=%async_computation.3 | async-start | bytes 1179648 | tf_op jit(solution)/shard_map/all_gather | solution.py:15
  8.2 149.5 %reduce-scatter.2.cloned.1.call-start = ((), (), s32[]{:S(2)}) async-start(), calls=%async_computation.1 | async-start | bytes 8650752 | tf_op jit(solution)/shard_map/reduce_scatter | solution.py:21
  55.5 157.7 %all-gather.4.cloned.1.call-start = ((), (), s32[]{:S(2)}) async-start(), calls=%async_computation.2 | async-start | bytes 4325376 | tf_op jit(solution)/shard_map/all_gather | solution.py:25
Sparse Core Ops, SparseCore 0:
  9.1 37.1 all-gather.5
  55.6 102.0 reduce-scatter.1
  160.7 52.5 all-gather.3

commit v2 on v1

v2 whole, which is shorter than its diff:
```python
import math

import jax
import jax.numpy as jnp
from jax import lax
from jax.sharding import PartitionSpec as P


def per_device(train_depth, train_basis, sample_basis, gram_inverse):
    terms_here = train_basis.shape[1]
    runs_here = train_basis.shape[0]
    n_cells = lax.axis_size("cells")
    total_runs = train_depth.shape[0] * lax.axis_size("runs")
    norm_scale = 1.0 / math.sqrt(total_runs)
    both = jnp.concatenate([train_basis, sample_basis], axis=1)
    both_full = lax.all_gather(both, "cells", axis=1, tiled=False)
    train_full = both_full[:, :, :terms_here].reshape(runs_here, n_cells * terms_here)
    sample_full = both_full[:, :, terms_here:].reshape(runs_here, n_cells * terms_here)
    folded = lax.dot_general(
        train_full.astype(jnp.float32), gram_inverse, (((1,), (1,)), ((), ())),
        precision=lax.Precision.HIGHEST,
    )
    folded_hi = folded.astype(jnp.bfloat16)
    folded_lo = (folded - folded_hi.astype(jnp.float32)).astype(jnp.bfloat16)
    dims = (((0,), (0,)), ((), ()))
    partial_t = lax.dot_general(
        train_depth, folded_hi, dims, preferred_element_type=jnp.float32
    ) + lax.dot_general(train_depth, folded_lo, dims, preferred_element_type=jnp.float32)
    coeffs_t = (lax.psum(partial_t, "runs") * norm_scale).astype(jnp.bfloat16)
    peak_depth = lax.dot_general(
        sample_full, coeffs_t, (((1,), (1,)), ((), ())), preferred_element_type=jnp.float32
    ).astype(jnp.bfloat16)
    return peak_depth


def solution(mesh):
    in_specs = (P("runs", "cells"), P("runs", "cells"), P("runs", "cells"), P())
    out_specs = P("runs", "cells")
    return jax.shard_map(
        per_device, mesh=mesh, in_specs=in_specs, out_specs=out_specs, check_vma=False
    )
```

time: 227 us -> 208 us (0.916)
  waiting for transfers between devices: 193 us -> 172 us
    psum x0 -> x1, waiting for transfers between devices: none -> 134 us  [per_device(): coeffs_t = (lax.psum(partial_t, 'runs') * norm_scale).astype(jnp.bfloat16)]
    reduce_scatter x1 -> x0, waiting for transfers between devices: 102 us -> none  [per_device(): lax.psum_scatter(partial_t, 'runs', scatter_dimension=0, tiled=True)]
    all_gather x2 -> x1, waiting for transfers between devices: 90.8 us -> 38.1 us  [per_device(): both_full = lax.all_gather(both, 'cells', axis=1, tiled=False)]
    dot_general x3 -> x4, matrix products: 17.3 us -> 19.5 us  [the longest x1 7.77 us: per_device(): lax.dot_general(sample_full, coeffs_t, (((1,), (1,)), ((), ())), preferre...]
  transfers between devices with their start and end apart: 3 -> 2, of which waited for: 3 -> 2; matrix products, arithmetic and copies ran while one was open for 0% -> 0% of each run, Pallas kernels for 0% -> 0%
where the time goes in v2:
time: 208 us
  waiting for transfers between devices  172 us (83%)
  matrix products  19.5 us (9%)
  between operations  13.4 us (6%)
    psum x1, waiting for transfers between devices, per_device(): coeffs_t = (lax.psum(partial_t, 'runs') * norm_scale).astype(jnp.bfloat16)  134 us
    all_gather x1, waiting for transfers between devices, per_device(): both_full = lax.all_gather(both, 'cells', axis=1, tiled=False)  38.1 us
    dot_general x1, matrix products, per_device(): lax.dot_general(sample_full, coeffs_t, (((1,), (1,)), ((), ())), preferre...  7.77 us
    dot_general x1, matrix products, per_device(): lax.dot_general(train_depth, folded_lo, dims, preferred_element_type=jnp....  5.83 us
    dot_general x1, matrix products, per_device(): lax.dot_general(train_depth, folded_hi, dims, preferred_element_type=jnp....  4.67 us
  transfers between devices with their start and end apart: 2, of which 2 were waited for; matrix products, arithmetic and copies ran while one was open for 0% of the time, Pallas kernels for 0%

profile of v2, /device:TPU:1, one launch (start us, length us, event | category | flops | bytes accessed | tf_op | source)
XLA Modules:
  0.0 207.7 jit_solution(90324181885658483)
XLA Ops:
  6.5 0.0 copy-start
  6.5 0.0 all-gather.3.cloned.1.call-start
  6.5 1.6 pad_maximum_fusion
  8.2 0.0 all-gather.3.cloned.1.call-update
  8.2 0.0 all-reduce.2.cloned.1.call-start
  8.2 38.1 %all-gather.3.cloned.1.call-done = bf16[512,1024]{0,1:T(8,128)(2,1)} async-done(((bf16[512,128]{0,1:T(8,128)(2,1)}), bf16[512,1024]{0,1:T(8,128)(2,1)}) %all-gather.3.cloned.1.call-update) | async-done | bytes 1048592 | tf_op jit(solution)/shard_map/all_gather | solution.py:16
  46.3 1.3 fusion.5
  47.6 0.0 copy-start.1
  47.6 0.0 copy-done
  47.6 1.2 fusion.6
  48.9 4.7 %fusion.2 = f32[512,4096]{1,0:T(8,128)S(1)} fusion(bf16[512,4096]{1,0:T(8,128)(2,1)} %param.4, f32[512,512]{1,0:T(8,128)S(1)} %fusion.6), kind=kOutput, calls=%fused_computation.6 | convolution fusion | flops 2147745792 | bytes 13631488 | tf_op jit(solution)/shard_map/dot_general | solution.py:26
  53.6 0.0 copy-done.1
  53.6 5.8 %add_bitcast_fusion = f32[4096,512]{0,1:T(8,128)} fusion(f32[512,4096]{1,0:T(8,128)S(1)} %fusion.2, bf16[512,4096]{1,0:T(8,128)(2,1)S(1)} %copy-done.1, f32[512,512]{1,0:T(8,128)S(1)} %fusion.6), kind=kOutput, calls=%fused_computation.1 | convolution fusion | flops 2150629376 | bytes 22020096 | tf_op jit(solution)/shard_map/dot_general | solution.py:28
  59.4 0.0 all-reduce.2.cloned.1.call-update
  59.4 133.7 %all-reduce.2.cloned.1.call-done = f32[4096,512]{0,1:T(8,128)} async-done(((f32[4096,512]{0,1:T(8,128)}), f32[4096,512]{0,1:T(8,128)}) %all-reduce.2.cloned.1.call-update) | async-done | bytes 8388624 | tf_op jit(solution)/shard_map/psum | solution.py:29
  193.1 7.8 %convolution_convert_fusion = bf16[512,4096]{1,0:T(8,128)(2,1)} fusion(bf16[512,512]{0,1:T(8,128)(2,1)S(1)} %bitcast.10, f32[4096,512]{0,1:T(8,128)} %all-reduce.2.cloned.1.call-done), kind=kOutput, calls=%fused_computation.2 | convolution fusion | flops 2153775104 | bytes 13107200 | tf_op jit(solution)/shard_map/dot_general | solution.py:30
Async XLA Ops:
  6.5 41.1 %copy-start = (f32[512,512]{1,0:T(8,128)S(1)}, f32[512,512]{1,0:T(8,128)}, u32[]{:S(2)}) copy-start(f32[512,512]{1,0:T(8,128)} %param.7) | copy-start | bytes 3145732
  6.5 39.8 %all-gather.3.cloned.1.call-start = ((), (), s32[]{:S(2)}) async-start(), calls=%async_computation.1 | async-start | bytes 1179648 | tf_op jit(solution)/shard_map/all_gather | solution.py:16
  8.2 184.9 %all-reduce.2.cloned.1.call-start = ((), (), s32[]{:S(2)}) async-start(), calls=%async_computation | async-start | bytes 16777216 | tf_op jit(solution)/shard_map/psum | solution.py:29
  47.6 5.9 %copy-start.1 = (bf16[512,4096]{1,0:T(8,128)(2,1)S(1)}, bf16[512,4096]{1,0:T(8,128)(2,1)}, u32[]{:S(2)}) copy-start(bf16[512,4096]{1,0:T(8,128)(2,1)} %param.4) | copy-start | bytes 12582916
Sparse Core Ops, SparseCore 0:
  9.1 37.1 all-gather.2
  59.5 133.5 all-reduce.1
